TPU v7x, 128 devices: a whole 4x4x4 slice. The times are simulated.
128 devices in a mesh: row: 8 (over x, core), col: 16 (over y, z).
Axes of the slice: x: 4, y: 4, z: 4, core: 2. Of those that a mesh axis runs over, the one named last changes fastest.
Arguments:
- front_matrix: float32 [16384, 16384], P('row', 'col'), may hold values from -2.5 to 202.5, as said below
- child_schur: float32 [2, 8192, 8192], P(None, 'row', 'col'), may hold values from -1.25 to 1.25
- child_index: int32 [2, 128], replicated, may hold values from 0 to 255, as said below
- child_valid: int32 [2, 128], replicated, may hold values 0 or 1
Outputs:
- trailing: float32 [16384, 16384], P('row', 'col')
- panel_factor: float32 [16384, 512], P('row')
Inputs may be any that keep to these rules, and one draw needn't show every extreme that they name: `front_matrix`: off the logical diagonal the entries lie in -2.5 to 2.5, on it in 97.5 to 202.5. `child_index`: each child's 128 entries are distinct front blocks. Among the child blocks a that share a mod 8, exactly 2 land in front blocks of each value mod 8; among the child blocks b that share b mod 16, at most 1 land in front blocks of any one value mod 16, and some value takes exactly 1.
All inputs are finite; a program needn't handle non-finite values.
Results may differ from a plain program's by a relative error of at most 0.00005.
Values sent between devices are 32-bit elements; how exact they have to be, the bound alone decides.
No kernel may reach another device: no remote copies, remote signals or barrier semaphores. Data moves between devices by JAX's collectives and lax.ppermute only.
A program may use at most 256 MiB of HBM per device.

v0:
```python
import jax
import jax.numpy as jnp
from jax import lax
from jax.sharding import PartitionSpec as P

CHILD = 8192
PANEL = 512
BLK = 64
exact_mode = lax.Precision.HIGHEST


def take_slabs(source, indices):
    return jnp.take(source, indices, axis=0)


def on_device(front_matrix, child_schur, child_index, child_valid):
    row_count = lax.axis_size("row")
    col_count = lax.axis_size("col")
    row_place = lax.axis_index("row")
    col_place = lax.axis_index("col")
    local_rows, local_cols = front_matrix.shape
    row_blocks = local_rows // BLK
    col_blocks = local_cols // BLK
    child_blocks = CHILD // BLK
    child_rowblk = child_schur.shape[1] // BLK
    child_colblk = child_schur.shape[2] // BLK
    per_owner = child_blocks // (row_count * row_count)
    col_multi = max(1, child_blocks // (col_count * col_count))
    row_slots = row_count * per_owner
    col_slots = col_count * col_multi
    validity = child_valid.astype(jnp.float32)
    all_blocks = jnp.arange(child_blocks)
    owner_row = child_index % row_count
    owner_col = child_index % col_count
    sender_row = all_blocks % row_count
    sender_col = all_blocks % col_count
    before = all_blocks[None, :] < all_blocks[:, None]
    earlier_row = (sender_row[:, None] == sender_row[None, :]) & before
    earlier_col = (sender_col[:, None] == sender_col[None, :]) & before
    row_rank = jnp.sum(
        (earlier_row[None] & (owner_row[:, :, None] == owner_row[:, None, :])).astype(jnp.int32),
        axis=2,
    )
    col_rank = jnp.sum(
        (earlier_col[None] & (owner_col[:, :, None] == owner_col[:, None, :])).astype(jnp.int32),
        axis=2,
    )
    row_key = owner_row * per_owner + row_rank
    col_key = owner_col * col_multi + col_rank
    local_arow = row_place + row_count * jnp.arange(child_rowblk)
    mine_rowkey = jnp.take(row_key, local_arow, axis=1)
    row_hit_send = mine_rowkey[:, :, None] == jnp.arange(row_slots)[None, None, :]
    src_row = jnp.sum(
        row_hit_send.astype(jnp.int32) * jnp.arange(child_rowblk)[None, :, None], axis=1
    )
    local_bcol = col_place + col_count * jnp.arange(child_colblk)
    mine_colkey = jnp.take(col_key, local_bcol, axis=1)
    col_hit_send = mine_colkey[:, :, None] == jnp.arange(col_slots)[None, None, :]
    src_col = jnp.sum(
        col_hit_send.astype(jnp.int32) * jnp.arange(child_colblk)[None, :, None], axis=1
    )
    has_col = jnp.sum(col_hit_send.astype(jnp.float32), axis=1)
    blocks = child_schur.reshape(2, child_rowblk, BLK, child_colblk * BLK)
    outgoing = jax.vmap(take_slabs)(blocks, src_row)
    outgoing = outgoing.reshape(2, row_slots * BLK, child_colblk * BLK)
    section_one = lax.all_to_all(outgoing, "row", split_axis=1, concat_axis=1, tiled=True)
    flipped = jnp.swapaxes(section_one, 1, 2).reshape(2, child_colblk, BLK, row_slots * BLK)
    onward = jax.vmap(take_slabs)(flipped, src_col) * has_col[:, :, None, None]
    onward = onward.reshape(2, col_slots * BLK, row_slots * BLK)
    section_two = lax.all_to_all(onward, "col", split_axis=1, concat_axis=1, tiled=True)
    arrived = section_two.reshape(2, col_slots, BLK, row_slots * BLK)
    front_rowblk = row_place + row_count * jnp.arange(row_blocks)
    match_rows = (child_index[:, None, :] == front_rowblk[None, :, None]).astype(jnp.int32)
    row_slot_of = sender_row[None, :] * per_owner + row_rank
    row_source = jnp.sum(match_rows * row_slot_of[:, None, :], axis=2)
    row_weight = jnp.sum(match_rows.astype(jnp.float32) * validity[:, None, :], axis=2)
    front_colblk = col_place + col_count * jnp.arange(col_blocks)
    match_cols = (child_index[:, None, :] == front_colblk[None, :, None]).astype(jnp.int32)
    col_slot_of = sender_col[None, :] * col_multi + col_rank
    col_source = jnp.sum(match_cols * col_slot_of[:, None, :], axis=2)
    col_weight = jnp.sum(match_cols.astype(jnp.float32) * validity[:, None, :], axis=2)
    by_col = jax.vmap(take_slabs)(arrived, col_source) * col_weight[:, :, None, None]
    by_col = by_col.reshape(2, local_cols, row_slots * BLK)
    unflipped = jnp.swapaxes(by_col, 1, 2).reshape(2, row_slots, BLK, local_cols)
    placed = jax.vmap(take_slabs)(unflipped, row_source) * row_weight[:, :, None, None]
    placed = placed.reshape(2, local_rows, local_cols)
    extended = front_matrix + placed[0] + placed[1]
    panel_width = PANEL // BLK
    spread = col_count // panel_width
    lead = extended[:, :BLK]
    lifted = lax.ppermute(
        lead,
        "col",
        [(c, c + panel_width * s) for s in range(1, spread) for c in range(panel_width)],
    )
    mine = jnp.where(col_place < panel_width, lead, lifted)
    part_rows = local_rows // spread
    part = lax.dynamic_slice_in_dim(mine, col_place // panel_width * part_rows, part_rows, axis=0)
    gathered = lax.all_gather(part, "col", axis=0, tiled=False)
    gathered = gathered.reshape(spread, panel_width, part_rows, BLK)
    panel_cols = gathered.transpose(0, 2, 1, 3).reshape(local_rows, PANEL)
    corner = lax.all_gather(panel_cols[: PANEL // row_count], "row", axis=0, tiled=True)
    lower_factor = jnp.linalg.cholesky(corner)
    solved = jax.scipy.linalg.solve_triangular(lower_factor, panel_cols.T, lower=True).T
    logical_blk = jnp.arange(row_blocks) * row_count + row_place
    factor_blocks = lower_factor.reshape(panel_width, BLK, PANEL)
    picked = jnp.take(factor_blocks, jnp.minimum(logical_blk, panel_width - 1), axis=0)
    in_panel = (logical_blk < panel_width)[:, None, None]
    panel_factor = jnp.where(in_panel, picked, solved.reshape(row_blocks, BLK, PANEL)).reshape(
        local_rows, PANEL
    )
    ratio = col_count // row_count
    arranged = panel_factor.reshape(col_blocks, ratio, BLK, PANEL)
    chosen = lax.dynamic_index_in_dim(arranged, col_place // row_count, axis=1, keepdims=False)
    chosen = chosen.reshape(col_blocks * BLK, PANEL)
    pairs = []
    for r0 in range(row_count):
        for c1 in range(col_count):
            dest_row = c1 % row_count
            dest_col = r0 + row_count * (c1 // row_count)
            pairs.append((r0 * col_count + c1, dest_row * col_count + dest_col))
    across = lax.ppermute(chosen, ("row", "col"), pairs)
    update = jnp.einsum("rp,cp->rc", panel_factor, across, precision=exact_mode)
    logical_row = jnp.arange(local_rows) // BLK * row_count + row_place
    logical_col = jnp.arange(local_cols) // BLK * col_count + col_place
    retained = (logical_row >= panel_width)[:, None] & (logical_col >= panel_width)[None, :]
    trailing = jnp.where(retained, extended - update, jnp.zeros_like(update))
    return (trailing, panel_factor)


def solution(mesh):
    in_specs = (P("row", "col"), P(None, "row", "col"), P(), P())
    out_specs = (P("row", "col"), P("row", None))
    return jax.shard_map(
        on_device, mesh=mesh, in_specs=in_specs, out_specs=out_specs, check_vma=False
    )
```

profile of v0, /device:TPU:7, one launch (start us, length us, event | category | flops | bytes accessed | tf_op | source)
XLA Modules:
  0.0 768.0 jit_solution(1678104543497816341)
XLA Ops:
  10.7 5.0 gather_fusion.3
  15.7 2.5 bitcast_select_fusion.2
  18.2 5.2 copy.126
  23.4 5.1 all-to-all-start
  29.0 46.6 %all-to-all-done = f32[2,1024,512]{2,0,1:T(2,128)} async-done(((f32[2,1024,512]{2,0,1:T(2,128)}), f32[2,1024,512]{2,0,1:T(2,128)}, u32[]{:S(2)}, u32[]{:S(2)}) %all-to-all-start) | async-done | bytes 4194336 | tf_op jit(solution)/shard_map/all_to_all | solution.py:66
  75.6 7.2 copy.127
  82.8 6.7 gather_fusion.4
  89.5 3.9 fusion.2
  93.4 12.9 %copy.128 = f32[2,1024,1024]{2,0,1:T(2,128)} copy(f32[2,1024,1024]{2,1,0:T(8,128)S(1)} %fusion.2) | data formatting | bytes 16777216 | tf_op jit(solution)/shard_map/mul | solution.py:68
  106.3 8.1 %all-to-all-start.1 = ((f32[2,1024,1024]{2,0,1:T(2,128)}), f32[2,1024,1024]{2,0,1:T(2,128)}, u32[]{:S(2)}, u32[]{:S(2)}) async-start(f32[2,1024,1024]{2,0,1:T(2,128)} %copy.128), calls=%async_computation.1 | async-start | bytes 16777216 | tf_op jit(solution)/shard_map/all_to_all | solution.py:70
  115.9 140.9 %all-to-all-done.1 = f32[2,1024,1024]{2,0,1:T(2,128)} async-done(((f32[2,1024,1024]{2,0,1:T(2,128)}), f32[2,1024,1024]{2,0,1:T(2,128)}, u32[]{:S(2)}, u32[]{:S(2)}) %all-to-all-start.1) | async-done | bytes 8388640 | tf_op jit(solution)/shard_map/all_to_all | solution.py:70
  256.8 9.5 %copy.129 = f32[2,1024,1024]{2,1,0:T(8,128)} copy(f32[2,1024,1024]{2,0,1:T(2,128)} %all-to-all-done.1) | data formatting | bytes 16777216 | tf_op jit(solution)/shard_map/all_to_all | solution.py:70
  266.3 7.7 %gather_fusion.5 = f32[32,64,1024]{2,1,0:T(8,128)} fusion(f32[2,16,64,1024]{3,2,1,0:T(8,128)} %bitcast.129, s32[32]{0:T(128)S(1)} %reshape.535), kind=kCustom, calls=%fused_computation.5 | custom fusion | bytes 16777472 | tf_op jit(solution)/shard_map/vmap(jit(_take))/gather | solution.py:13
  274.0 6.0 fusion.1
  280.0 8.7 %copy.130 = f32[2,1024,1024]{2,1,0:T(8,128)} copy(f32[2,1024,1024]{1,2,0:T(8,128)} %fusion.1) | data formatting | bytes 16777216 | tf_op jit(solution)/shard_map/transpose | solution.py:84
  288.7 12.5 %gather_fusion.6 = f32[64,64,1024]{2,1,0:T(8,128)} fusion(f32[2,16,64,1024]{3,2,1,0:T(8,128)} %bitcast.124, s32[64]{0:T(128)S(1)} %reshape.541), kind=kCustom, calls=%fused_computation.6 | custom fusion | bytes 33554944 | tf_op jit(solution)/shard_map/vmap(jit(_take))/gather | solution.py:13
  301.2 7.3 select_multiply_fusion
  308.5 6.7 fusion.77
  315.2 9.7 %bitcast_add_fusion = f32[2048,1024]{1,0:T(8,128)S(1)} fusion(f32[1,32,64,1024]{3,2,1,0:T(8,128)} %get-tuple-element.35, f32[2048,1024]{1,0:T(8,128)} %param.4, f32[1,32,64,1024]{3,2,1,0:T(8,128)} %get-tuple-element.34), kind=kLoop, calls=%fused_computation.10 | loop fusion | flops 4194304 | bytes 33554432 | tf_op jit(solution)/shard_map/add | solution.py:87
  325.0 3.4 copy-done
  328.8 1.3 collective-permute-start
  330.2 8.5 %collective-permute-done = f32[2048,64]{0,1:T(8,128)S(1)} collective-permute-done((f32[2048,64]{0,1:T(8,128)S(1)}, f32[2048,64]{0,1:T(8,128)S(1)}, u32[]{:S(2)}, u32[]{:S(2)}) %collective-permute-start) | collective-permute-done | bytes 524320 | tf_op jit(solution)/shard_map/ppermute | solution.py:91
  338.9 0.9 dynamic-slice_select_fusion.2
  339.9 84.5 %all-gather.6.cloned.1.call-done = f32[16384,64]{1,0:T(8,128)} async-done(((f32[1024,64]{1,0:T(8,128)}), f32[16384,64]{1,0:T(8,128)}) %all-gather.6.cloned.1.call-update) | async-done | bytes 4194320 | tf_op jit(solution)/shard_map/all_gather | solution.py:99
  424.4 9.0 %copy.133 = f32[2,8,1024,64]{2,0,3,1:T(2,128)} copy(f32[2,8,1024,64]{3,2,1,0:T(8,128)} %bitcast.141) | data formatting | bytes 8388608 | tf_op jit(solution)/shard_map/reshape | solution.py:100
  433.4 4.1 copy.142
  437.6 2.0 copy-done.1
  439.6 0.8 copy.134
  440.8 21.5 %all-gather.4.cloned.1.call-done = f32[512,512]{1,0:T(8,128)} async-done(((f32[64,512]{1,0:T(8,128)}), f32[512,512]{1,0:T(8,128)}) %all-gather.4.cloned.1.call-update) | async-done | bytes 1048592 | tf_op jit(solution)/shard_map/all_gather | solution.py:102
  462.3 1.6 copy.135
  463.9 1.4 fusion.17
  465.3 11.7 %cholesky.104 = f32[128,128]{1,0:T(8,128)S(1)} custom-call(f32[128,128]{1,0:T(8,128)S(1)} %cholesky.266), custom_call_target="Cholesky" | custom-call | tf_op jit(solution)/shard_map/jit(cholesky)/cholesky | solution.py:103
  477.2 9.8 %custom-call.31 = f32[1,128,128]{1,2,0:T(8,128)S(1)} custom-call(f32[1,128,128]{2,1,0:T(8,128)S(1)} %get-tuple-element.45), custom_call_target="InvertDiagBlocksLowerTriangular" | custom-call | tf_op jit(solution)/shard_map/jit(cholesky)/cholesky | solution.py:103
  487.7 11.9 %cholesky.217 = f32[128,128]{1,0:T(8,128)S(1)} custom-call(f32[128,128]{1,0:T(8,128)S(1)} %cholesky.270), custom_call_target="Cholesky" | custom-call | tf_op jit(solution)/shard_map/jit(cholesky)/cholesky | solution.py:103
  500.2 0.7 compare_reduce_fusion.3
  500.9 9.8 %custom-call.32 = f32[1,128,128]{1,2,0:T(8,128)S(1)} custom-call(f32[1,128,128]{2,1,0:T(8,128)S(1)} %get-tuple-element.42), custom_call_target="InvertDiagBlocksLowerTriangular" | custom-call | tf_op jit(solution)/shard_map/jit(cholesky)/cholesky | solution.py:103
  511.4 11.7 %cholesky.238 = f32[128,128]{1,0:T(8,128)S(1)} custom-call(f32[128,128]{1,0:T(8,128)S(1)} %cholesky.275), custom_call_target="Cholesky" | custom-call | tf_op jit(solution)/shard_map/jit(cholesky)/cholesky | solution.py:103
  523.8 9.8 %custom-call.33 = f32[1,128,128]{1,2,0:T(8,128)S(1)} custom-call(f32[1,128,128]{2,1,0:T(8,128)S(1)} %get-tuple-element.39), custom_call_target="InvertDiagBlocksLowerTriangular" | custom-call | tf_op jit(solution)/shard_map/jit(cholesky)/cholesky | solution.py:103
  534.2 11.9 %cholesky.255 = f32[128,128]{1,0:T(8,128)S(1)} custom-call(f32[128,128]{1,0:T(8,128)S(1)} %convolution_subtract_fusion.4), custom_call_target="Cholesky" | custom-call | tf_op jit(solution)/shard_map/jit(cholesky)/cholesky | solution.py:103
  546.2 0.7 compare_reduce_fusion
  549.7 10.5 %while.1 = (s32[]{:T(128)}, f32[512,512]{1,0:T(8,128)S(1)}, s32[4,2]{0,1:T(2,128)S(1)}, f32[4,128,128]{2,1,0:T(8,128)}, s32[]{:T(128)}) while((s32[]{:T(128)}, f32[512,512]{1,0:T(8,128)S(1)}, s32[4,2]{0,1:T(2,128)S(1)}, f32[4,128,128]{2,1,0:T(8,128)}, s32[]{:T(128)}) %tuple.44), condition=%wide.while_cond, body=%wide.while_body.sunk | while | flops 2 | bytes 132705 | solution.py:104
  550.4 2.0 bitcast_dynamic-update-slice_fusion.2
  553.0 2.0 bitcast_dynamic-update-slice_fusion.2
  555.6 2.0 bitcast_dynamic-update-slice_fusion.2
  558.3 2.0 bitcast_dynamic-update-slice_fusion.2
  560.2 40.2 %custom-call.34 = f32[4,128,128]{1,2,0:T(8,128)S(1)} custom-call(f32[4,128,128]{2,1,0:T(8,128)} %get-tuple-element.9), custom_call_target="InvertDiagBlocksLowerTriangular" | custom-call | tf_op jit(solution)/shard_map/jit(_solve_triangular)/triangular_solve | solution.py:104
  600.4 2.4 fusion.15
  602.8 2.2 convolution_subtract_fusion.1
  605.1 1.1 fusion.30
  606.2 2.2 convolution_subtract_fusion
  608.3 1.1 fusion.28
  609.4 3.2 fusion.9
  612.6 1.0 fusion.27
  613.7 1.1 copy-done.5
  614.7 2.4 maximum_bitcast_fusion
  617.1 5.3 copy.139
  622.5 2.8 gather_fusion.2
  625.3 4.2 dynamic-slice_select_fusion
  629.5 7.2 collective-permute-start.1
  637.1 5.7 copy.136
  642.8 5.4 select_select_fusion
  648.2 5.3 copy.140
  653.5 75.5 %collective-permute-done.1 = f32[1024,512]{1,0:T(8,128)} collective-permute-done((f32[1024,512]{1,0:T(8,128)}, f32[1024,512]{1,0:T(8,128)}, u32[]{:S(2)}, u32[]{:S(2)}) %collective-permute-start.1) | collective-permute-done | bytes 2097184 | tf_op jit(solution)/shard_map/ppermute | solution.py:122
  729.1 31.7 %subtract_select_fusion = f32[2048,1024]{1,0:T(8,128)} fusion(f32[2048,1024]{1,0:T(8,128)} %copy-done, pred[1024]{0:T(1024)(128)(4,1)S(1)} %fusion.54, pred[2048]{0:T(1024)(128)(4,1)S(1)} %fusion.48, f32[2048,512]{0,1:T(8,128)} %select_select_fusion, f32[1024,512]{1,0:T(8,128)} %collective-permute-done.1), kind=kOutput, calls=%fused_computation.17 | convolution fusion | flops 12891193344 | bytes 23071744 | tf_op jit(solution)/shard_map/rp,cp->rc/dot_general | solution.py:123
  (121 shorter events, 13.3 us)
Async XLA Ops:
  23.4 52.2 %all-to-all-start = ((f32[2,1024,512]{2,0,1:T(2,128)}), f32[2,1024,512]{2,0,1:T(2,128)}, u32[]{:S(2)}, u32[]{:S(2)}) async-start(f32[2,1024,512]{2,0,1:T(2,128)} %copy.126), calls=%async_computation | async-start | bytes 8388608 | tf_op jit(solution)/shard_map/all_to_all | solution.py:66
  106.3 8.3 %copy-start.7 = (s32[2,128]{1,0:T(2,128)S(1)}, s32[2,128]{1,0:T(2,128)}, u32[]{:S(2)}) copy-start(s32[2,128]{1,0:T(2,128)} %param.6) | copy-start | bytes 3076
  106.3 8.8 %copy-start.8 = (s32[2,128]{1,0:T(2,128)S(1)}, s32[2,128]{1,0:T(2,128)}, u32[]{:S(2)}) copy-start(s32[2,128]{1,0:T(2,128)} %param.7) | copy-start | bytes 3076
  106.3 150.5 %all-to-all-start.1 = ((f32[2,1024,1024]{2,0,1:T(2,128)}), f32[2,1024,1024]{2,0,1:T(2,128)}, u32[]{:S(2)}, u32[]{:S(2)}) async-start(f32[2,1024,1024]{2,0,1:T(2,128)} %copy.128), calls=%async_computation.1 | async-start | bytes 16777216 | tf_op jit(solution)/shard_map/all_to_all | solution.py:70
  114.4 310.0 %all-gather.6.cloned.1.call-start = ((), (), s32[]{:S(2)}) async-start(), calls=%async_computation.3 | async-start | bytes 8912896 | tf_op jit(solution)/shard_map/all_gather | solution.py:99
  325.0 3.4 copy-start
  328.8 9.9 %collective-permute-start = (f32[2048,64]{0,1:T(8,128)S(1)}, f32[2048,64]{0,1:T(8,128)S(1)}, u32[]{:S(2)}, u32[]{:S(2)}) collective-permute-start(f32[2048,64]{0,1:T(8,128)S(1)} %copy.131), channel_id=1, source_target_pairs={{0,8},{1,9},{2,10},{3,11},{4,12},{5,13},{6,14},{7,15},{16,24},{17,... | collective-permute-start | bytes 1572872 | tf_op jit(solution)/shard_map/ppermute | solution.py:91
  339.8 122.5 %all-gather.4.cloned.1.call-start = ((), (), s32[]{:S(2)}) async-start(), calls=%async_computation.2 | async-start | bytes 1179648 | tf_op jit(solution)/shard_map/all_gather | solution.py:102
  437.6 2.0 copy-start.1
  560.2 42.6 %copy-start.6 = (f32[512,512]{1,0:T(8,128)}, f32[512,512]{1,0:T(8,128)S(1)}, u32[]{:S(2)}) copy-start(f32[512,512]{1,0:T(8,128)S(1)} %get-tuple-element.112) | copy-start | bytes 3145732
  600.4 5.7 copy-start.2
  609.4 4.2 copy-start.3
  613.7 1.1 copy-start.5
  629.5 99.5 %collective-permute-start.1 = (f32[1024,512]{1,0:T(8,128)}, f32[1024,512]{1,0:T(8,128)}, u32[]{:S(2)}, u32[]{:S(2)}) collective-permute-start(f32[1024,512]{1,0:T(8,128)} %bitcast.40), channel_id=1, source_target_pairs={{0,0},{1,16},{2,32},{3,48},{4,64},{5,80},{6,96},{7,112},{8,8},{9,2... | collective-permute-start | bytes 6291464 | tf_op jit(solution)/shard_map/ppermute | solution.py:122
  637.1 5.7 copy-start.4
Sparse Core Ops, SparseCore 0:
  339.9 84.4 all-gather.5
  440.5 21.7 all-gather.3
where the time goes:
time: 777 us; the launch traced here: 768 us
  waiting for transfers between devices  378 us (49%)
  other arithmetic  166 us (21%)
  local copies, waits for them, and re-layouts  138 us (18%)
  matrix products  46.7 us (6%)
  starting transfers between devices  22 us (3%)
  between operations  17.6 us (2%)
    all_to_all x1, waiting for transfers between devices, on_device(): lax.all_to_all(onward, 'col', split_axis=1, concat_axis=1, tiled=True)  141 us
    all_gather x1, waiting for transfers between devices, on_device(): gathered = lax.all_gather(part, 'col', axis=0, tiled=False)  84.5 us
    another operation x15, other arithmetic, on_device(): lower_factor = jnp.linalg.cholesky(corner)  79.5 us
    ppermute x1, waiting for transfers between devices, on_device(): across = lax.ppermute(chosen, ('row', 'col'), pairs)  75.5 us
    all_to_all x1, waiting for transfers between devices, on_device(): lax.all_to_all(outgoing, 'row', split_axis=1, concat_axis=1, tiled=True)  46.6 us
    another operation x3, other arithmetic, on_device(): jax.scipy.linalg.solve_triangular(lower_factor, panel_cols.T, lower=True)  40.4 us
    gather x8, local copies, waits for them, and re-layouts, take_slabs(): return jnp.take(source, indices, axis=0)  32.2 us
    dot_general x1, matrix products, on_device(): update = jnp.einsum('rp,cp->rc', panel_factor, across, precision=exact_mode)  31.7 us
  transfers between devices with their start and end apart: 6, of which 6 were waited for; matrix products, arithmetic and copies ran while one was open for 2% of the time, Pallas kernels for 0%

commit v1 on v0

--- a/solution.py
+++ b/solution.py
@@ -63,7 +63,10 @@
     blocks = child_schur.reshape(2, child_rowblk, BLK, child_colblk * BLK)
     outgoing = jax.vmap(take_slabs)(blocks, src_row)
     outgoing = outgoing.reshape(2, row_slots * BLK, child_colblk * BLK)
-    section_one = lax.all_to_all(outgoing, "row", split_axis=1, concat_axis=1, tiled=True)
+    section_one = jnp.concatenate(
+        lax.all_to_all(jnp.stack(jnp.split(outgoing, lax.axis_size("row"), axis=1)), "row", 0, 0),
+        axis=1,
+    )
     flipped = jnp.swapaxes(section_one, 1, 2).reshape(2, child_colblk, BLK, row_slots * BLK)
     onward = jax.vmap(take_slabs)(flipped, src_col) * has_col[:, :, None, None]
     onward = onward.reshape(2, col_slots * BLK, row_slots * BLK)

time: 777 us -> 779 us (level)
    unnamed x21 -> x28, local copies, waits for them, and re-layouts: 16.2 us -> 22 us
where the time goes in v1:
time: 779 us; the launch traced here: 772 us
  waiting for transfers between devices  378 us (49%)
  other arithmetic  166 us (21%)
  local copies, waits for them, and re-layouts  142 us (18%)
  matrix products  46.7 us (6%)
  starting transfers between devices  22 us (3%)
  between operations  17.6 us (2%)
    all_to_all x1, waiting for transfers between devices, on_device(): lax.all_to_all(onward, 'col', split_axis=1, concat_axis=1, tiled=True)  141 us
    all_gather x1, waiting for transfers between devices, on_device(): gathered = lax.all_gather(part, 'col', axis=0, tiled=False)  84.5 us
    another operation x15, other arithmetic, on_device(): lower_factor = jnp.linalg.cholesky(corner)  79.5 us
    ppermute x1, waiting for transfers between devices, on_device(): across = lax.ppermute(chosen, ('row', 'col'), pairs)  75.5 us
    all_to_all x1, waiting for transfers between devices, on_device(): lax.all_to_all(jnp.stack(jnp.split(outgoing, lax.axis_size('row'), axis=1...  46.6 us
    another operation x3, other arithmetic, on_device(): jax.scipy.linalg.solve_triangular(lower_factor, panel_cols.T, lower=True)  40.4 us
    gather x8, local copies, waits for them, and re-layouts, take_slabs(): return jnp.take(source, indices, axis=0)  32.2 us
    dot_general x1, matrix products, on_device(): update = jnp.einsum('rp,cp->rc', panel_factor, across, precision=exact_mode)  31.7 us
  transfers between devices with their start and end apart: 6, of which 6 were waited for; matrix products, arithmetic and copies ran while one was open for 2% of the time, Pallas kernels for 0%

profile of v1, /device:TPU:7, one launch (start us, length us, event | category | flops | bytes accessed | tf_op | source)
XLA Modules:
  0.0 772.4 jit_solution(8623027801980188069)
XLA Ops:
  10.7 5.0 gather_fusion.3
  15.7 2.5 bitcast_select_fusion.2
  18.2 0.8 fusion.26
  19.0 0.8 fusion.25
  19.8 0.8 fusion.24
  24.8 5.1 all-to-all-start
  30.4 46.6 %all-to-all-done = f32[8,2,128,512]{3,2,1,0:T(8,128)} async-done(((f32[8,2,128,512]{3,2,1,0:T(8,128)}), f32[8,2,128,512]{3,2,1,0:T(8,128)}, u32[]{:S(2)}, u32[]{:S(2)}) %all-to-all-start) | async-done | bytes 4194336 | tf_op jit(solution)/shard_map/all_to_all | solution.py:67
  77.0 4.8 copy.141
  81.8 5.4 copy.142
  87.2 6.7 gather_fusion.4
  93.9 3.9 fusion.2
  97.8 12.9 %copy.143 = f32[2,1024,1024]{2,0,1:T(2,128)} copy(f32[2,1024,1024]{2,1,0:T(8,128)S(1)} %fusion.2) | data formatting | bytes 16777216 | tf_op jit(solution)/shard_map/mul | solution.py:71
  110.7 8.1 %all-to-all-start.1 = ((f32[2,1024,1024]{2,0,1:T(2,128)}), f32[2,1024,1024]{2,0,1:T(2,128)}, u32[]{:S(2)}, u32[]{:S(2)}) async-start(f32[2,1024,1024]{2,0,1:T(2,128)} %copy.143), calls=%async_computation.1 | async-start | bytes 16777216 | tf_op jit(solution)/shard_map/all_to_all | solution.py:73
  120.3 140.9 %all-to-all-done.1 = f32[2,1024,1024]{2,0,1:T(2,128)} async-done(((f32[2,1024,1024]{2,0,1:T(2,128)}), f32[2,1024,1024]{2,0,1:T(2,128)}, u32[]{:S(2)}, u32[]{:S(2)}) %all-to-all-start.1) | async-done | bytes 8388640 | tf_op jit(solution)/shard_map/all_to_all | solution.py:73
  261.2 9.5 %copy.144 = f32[2,1024,1024]{2,1,0:T(8,128)} copy(f32[2,1024,1024]{2,0,1:T(2,128)} %all-to-all-done.1) | data formatting | bytes 16777216 | tf_op jit(solution)/shard_map/all_to_all | solution.py:73
  270.7 7.7 gather_fusion.5
  278.4 6.0 fusion.1
  284.4 8.7 %copy.145 = f32[2,1024,1024]{2,1,0:T(8,128)} copy(f32[2,1024,1024]{1,2,0:T(8,128)} %fusion.1) | data formatting | bytes 16777216 | tf_op jit(solution)/shard_map/transpose | solution.py:87
  293.1 12.5 %gather_fusion.6 = f32[64,64,1024]{2,1,0:T(8,128)} fusion(f32[2,16,64,1024]{3,2,1,0:T(8,128)} %bitcast.159, s32[64]{0:T(128)S(1)} %reshape.549), kind=kCustom, calls=%fused_computation.6 | custom fusion | bytes 33554944 | tf_op jit(solution)/shard_map/vmap(jit(_take))/gather | solution.py:13
  305.6 7.3 select_multiply_fusion
  312.9 6.7 fusion.85
  319.6 9.7 %bitcast_add_fusion = f32[2048,1024]{1,0:T(8,128)S(1)} fusion(f32[1,32,64,1024]{3,2,1,0:T(8,128)} %get-tuple-element.35, f32[2048,1024]{1,0:T(8,128)} %param.4, f32[1,32,64,1024]{3,2,1,0:T(8,128)} %get-tuple-element.34), kind=kLoop, calls=%fused_computation.10 | loop fusion | flops 4194304 | bytes 33554432 | tf_op jit(solution)/shard_map/add | solution.py:90
  329.4 3.4 copy-done
  333.2 1.3 collective-permute-start
  334.6 8.5 %collective-permute-done = f32[2048,64]{0,1:T(8,128)S(1)} collective-permute-done((f32[2048,64]{0,1:T(8,128)S(1)}, f32[2048,64]{0,1:T(8,128)S(1)}, u32[]{:S(2)}, u32[]{:S(2)}) %collective-permute-start) | collective-permute-done | bytes 524320 | tf_op jit(solution)/shard_map/ppermute | solution.py:94
  343.4 0.9 dynamic-slice_select_fusion.2
  344.3 84.5 %all-gather.6.cloned.1.call-done = f32[16384,64]{1,0:T(8,128)} async-done(((f32[1024,64]{1,0:T(8,128)}), f32[16384,64]{1,0:T(8,128)}) %all-gather.6.cloned.1.call-update) | async-done | bytes 4194320 | tf_op jit(solution)/shard_map/all_gather | solution.py:102
  428.8 9.0 %copy.148 = f32[2,8,1024,64]{2,0,3,1:T(2,128)} copy(f32[2,8,1024,64]{3,2,1,0:T(8,128)} %bitcast.177) | data formatting | bytes 8388608 | tf_op jit(solution)/shard_map/reshape | solution.py:103
  437.8 4.1 copy.157
  442.0 2.0 copy-done.1
  445.2 21.5 %all-gather.4.cloned.1.call-done = f32[512,512]{1,0:T(8,128)} async-done(((f32[64,512]{1,0:T(8,128)}), f32[512,512]{1,0:T(8,128)}) %all-gather.4.cloned.1.call-update) | async-done | bytes 1048592 | tf_op jit(solution)/shard_map/all_gather | solution.py:105
  466.7 1.6 copy.150
  468.3 1.4 fusion.17
  469.7 11.7 %cholesky.104 = f32[128,128]{1,0:T(8,128)S(1)} custom-call(f32[128,128]{1,0:T(8,128)S(1)} %cholesky.266), custom_call_target="Cholesky" | custom-call | tf_op jit(solution)/shard_map/jit(cholesky)/cholesky | solution.py:106
  481.6 9.8 %custom-call.31 = f32[1,128,128]{1,2,0:T(8,128)S(1)} custom-call(f32[1,128,128]{2,1,0:T(8,128)S(1)} %get-tuple-element.45), custom_call_target="InvertDiagBlocksLowerTriangular" | custom-call | tf_op jit(solution)/shard_map/jit(cholesky)/cholesky | solution.py:106
  492.1 11.9 %cholesky.217 = f32[128,128]{1,0:T(8,128)S(1)} custom-call(f32[128,128]{1,0:T(8,128)S(1)} %cholesky.270), custom_call_target="Cholesky" | custom-call | tf_op jit(solution)/shard_map/jit(cholesky)/cholesky | solution.py:106
  505.4 9.8 %custom-call.32 = f32[1,128,128]{1,2,0:T(8,128)S(1)} custom-call(f32[1,128,128]{2,1,0:T(8,128)S(1)} %get-tuple-element.42), custom_call_target="InvertDiagBlocksLowerTriangular" | custom-call | tf_op jit(solution)/shard_map/jit(cholesky)/cholesky | solution.py:106
  515.8 11.7 %cholesky.238 = f32[128,128]{1,0:T(8,128)S(1)} custom-call(f32[128,128]{1,0:T(8,128)S(1)} %cholesky.275), custom_call_target="Cholesky" | custom-call | tf_op jit(solution)/shard_map/jit(cholesky)/cholesky | solution.py:106
  528.2 9.8 %custom-call.33 = f32[1,128,128]{1,2,0:T(8,128)S(1)} custom-call(f32[1,128,128]{2,1,0:T(8,128)S(1)} %get-tuple-element.39), custom_call_target="InvertDiagBlocksLowerTriangular" | custom-call | tf_op jit(solution)/shard_map/jit(cholesky)/cholesky | solution.py:106
  538.7 11.9 %cholesky.255 = f32[128,128]{1,0:T(8,128)S(1)} custom-call(f32[128,128]{1,0:T(8,128)S(1)} %convolution_subtract_fusion.4), custom_call_target="Cholesky" | custom-call | tf_op jit(solution)/shard_map/jit(cholesky)/cholesky | solution.py:106
  554.1 10.5 %while.1 = (s32[]{:T(128)}, f32[512,512]{1,0:T(8,128)S(1)}, s32[4,2]{0,1:T(2,128)S(1)}, f32[4,128,128]{2,1,0:T(8,128)}, s32[]{:T(128)}) while((s32[]{:T(128)}, f32[512,512]{1,0:T(8,128)S(1)}, s32[4,2]{0,1:T(2,128)S(1)}, f32[4,128,128]{2,1,0:T(8,128)}, s32[]{:T(128)}) %tuple.45), condition=%wide.while_cond, body=%wide.while_body.sunk | while | flops 2 | bytes 132705 | solution.py:107
  554.8 2.0 bitcast_dynamic-update-slice_fusion.2
  557.4 2.0 bitcast_dynamic-update-slice_fusion.2
  560.1 2.0 bitcast_dynamic-update-slice_fusion.2
  562.7 2.0 bitcast_dynamic-update-slice_fusion.2
  564.6 40.2 %custom-call.34 = f32[4,128,128]{1,2,0:T(8,128)S(1)} custom-call(f32[4,128,128]{2,1,0:T(8,128)} %get-tuple-element.9), custom_call_target="InvertDiagBlocksLowerTriangular" | custom-call | tf_op jit(solution)/shard_map/jit(_solve_triangular)/triangular_solve | solution.py:107
  604.8 2.4 fusion.15
  607.3 2.2 convolution_subtract_fusion.1
  609.5 1.1 fusion.38
  610.6 2.2 convolution_subtract_fusion
  612.8 1.1 fusion.36
  613.8 3.2 fusion.9
  617.0 1.0 fusion.35
  618.1 1.1 copy-done.5
  619.1 2.4 maximum_bitcast_fusion
  621.5 5.3 copy.154
  626.9 2.8 gather_fusion.2
  629.7 4.2 dynamic-slice_select_fusion
  633.9 7.2 collective-permute-start.1
  641.6 5.7 copy.151
  647.2 5.4 select_select_fusion
  652.6 5.3 copy.155
  657.9 75.5 %collective-permute-done.1 = f32[1024,512]{1,0:T(8,128)} collective-permute-done((f32[1024,512]{1,0:T(8,128)}, f32[1024,512]{1,0:T(8,128)}, u32[]{:S(2)}, u32[]{:S(2)}) %collective-permute-start.1) | collective-permute-done | bytes 2097184 | tf_op jit(solution)/shard_map/ppermute | solution.py:125
  733.4 31.7 %subtract_select_fusion = f32[2048,1024]{1,0:T(8,128)} fusion(f32[2048,1024]{1,0:T(8,128)} %copy-done, pred[1024]{0:T(1024)(128)(4,1)S(1)} %fusion.62, pred[2048]{0:T(1024)(128)(4,1)S(1)} %fusion.56, f32[2048,512]{0,1:T(8,128)} %select_select_fusion, f32[1024,512]{1,0:T(8,128)} %collective-permute-done.1), kind=kOutput, calls=%fused_computation.17 | convolution fusion | flops 12891193344 | bytes 23071744 | tf_op jit(solution)/shard_map/rp,cp->rc/dot_general | solution.py:126
  (128 shorter events, 19.6 us)
Async XLA Ops:
  24.8 52.2 %all-to-all-start = ((f32[8,2,128,512]{3,2,1,0:T(8,128)}), f32[8,2,128,512]{3,2,1,0:T(8,128)}, u32[]{:S(2)}, u32[]{:S(2)}) async-start(f32[8,2,128,512]{3,2,1,0:T(8,128)} %fusion.19), calls=%async_computation | async-start | bytes 8388608 | tf_op jit(solution)/shard_map/all_to_all | solution.py:67
  110.7 8.3 %copy-start.7 = (s32[2,128]{1,0:T(2,128)S(1)}, s32[2,128]{1,0:T(2,128)}, u32[]{:S(2)}) copy-start(s32[2,128]{1,0:T(2,128)} %param.6) | copy-start | bytes 3076
  110.7 8.8 %copy-start.8 = (s32[2,128]{1,0:T(2,128)S(1)}, s32[2,128]{1,0:T(2,128)}, u32[]{:S(2)}) copy-start(s32[2,128]{1,0:T(2,128)} %param.7) | copy-start | bytes 3076
  110.7 150.5 %all-to-all-start.1 = ((f32[2,1024,1024]{2,0,1:T(2,128)}), f32[2,1024,1024]{2,0,1:T(2,128)}, u32[]{:S(2)}, u32[]{:S(2)}) async-start(f32[2,1024,1024]{2,0,1:T(2,128)} %copy.143), calls=%async_computation.1 | async-start | bytes 16777216 | tf_op jit(solution)/shard_map/all_to_all | solution.py:73
  118.8 310.0 %all-gather.6.cloned.1.call-start = ((), (), s32[]{:S(2)}) async-start(), calls=%async_computation.3 | async-start | bytes 8912896 | tf_op jit(solution)/shard_map/all_gather | solution.py:102
  329.4 3.4 copy-start
  333.2 9.9 %collective-permute-start = (f32[2048,64]{0,1:T(8,128)S(1)}, f32[2048,64]{0,1:T(8,128)S(1)}, u32[]{:S(2)}, u32[]{:S(2)}) collective-permute-start(f32[2048,64]{0,1:T(8,128)S(1)} %copy.146), channel_id=1, source_target_pairs={{0,8},{1,9},{2,10},{3,11},{4,12},{5,13},{6,14},{7,15},{16,24},{17,... | collective-permute-start | bytes 1572872 | tf_op jit(solution)/shard_map/ppermute | solution.py:94
  344.2 122.5 %all-gather.4.cloned.1.call-start = ((), (), s32[]{:S(2)}) async-start(), calls=%async_computation.2 | async-start | bytes 1179648 | tf_op jit(solution)/shard_map/all_gather | solution.py:105
  442.0 2.0 copy-start.1
  564.6 42.6 %copy-start.6 = (f32[512,512]{1,0:T(8,128)}, f32[512,512]{1,0:T(8,128)S(1)}, u32[]{:S(2)}) copy-start(f32[512,512]{1,0:T(8,128)S(1)} %get-tuple-element.112) | copy-start | bytes 3145732
  604.8 5.7 copy-start.2
  613.8 4.2 copy-start.3
  618.1 1.1 copy-start.5
  633.9 99.5 %collective-permute-start.1 = (f32[1024,512]{1,0:T(8,128)}, f32[1024,512]{1,0:T(8,128)}, u32[]{:S(2)}, u32[]{:S(2)}) collective-permute-start(f32[1024,512]{1,0:T(8,128)} %bitcast.50), channel_id=1, source_target_pairs={{0,0},{1,16},{2,32},{3,48},{4,64},{5,80},{6,96},{7,112},{8,8},{9,2... | collective-permute-start | bytes 6291464 | tf_op jit(solution)/shard_map/ppermute | solution.py:125
  641.5 5.7 copy-start.4
Sparse Core Ops, SparseCore 0:
  344.4 84.4 all-gather.5
  444.9 21.7 all-gather.3
